TPU v7x, 512 devices: a whole 4x4x16 slice. The times are simulated.
512 devices in a mesh: section: 8 (over x, y_hi), vocab: 64 (over z, y_lo, core).
Axes of the slice: x: 4, y: 4 (y_hi: 2, y_lo: 2; y = y_hi * 2 + y_lo), z: 16, core: 2. Of those that a mesh axis runs over, the one named last changes fastest.
Arguments:
- hidden: bfloat16 [512, 8192], P('vocab', 'section'), may hold values from -6 to 6
- head_weight: bfloat16 [98304, 8192], P('vocab', 'section'), may hold values from -3 to 3
- lengths: int32 [8], replicated, may hold values from 16 to 64
- pairing: int32 [4], replicated, may hold values from 0 to 3, each once
Outputs:
- hidden_grad: float32 [512, 8192], P('vocab', 'section')
- loss: float32 [], replicated
Inputs may be any that keep to these rules, and one draw needn't show every extreme that they name: Every sequence has at least one live token; positions from lengths on are padding. `pairing`: a permutation: each document matches exactly one query.
All inputs are finite; a program needn't handle non-finite values.
Results may differ from a plain program's by a relative error of at most 0.0018.
Values may be sent and summed in bfloat16 or wider, within the bound.
No kernel may reach another device: no remote copies, remote signals or barrier semaphores. Data moves between devices by JAX's collectives and lax.ppermute only.
A program may use at most 64 MiB of HBM per device.

v0:
```python
import jax
import jax.numpy as jnp
from jax import lax
from jax.sharding import Mesh
from jax.sharding import PartitionSpec as P

NSEQ = 8
pool_temp = 0.5
score_temp = 0.02
grad_scale = 16.0
eps_norm = 1e-06
SEC = ("x", "yh")
VOC = ("z", "yl", "c")


def local(hidden, head_weight, lengths, pairing):
    half = NSEQ // 2
    gathered = lax.all_gather(hidden, ("yl", "c"), axis=0, tiled=True)
    gathered = lax.all_gather(gathered, "z", axis=0, tiled=True)
    partial_logits = lax.dot_general(
        gathered, head_weight, (((1,), (1,)), ((), ())), preferred_element_type=jnp.float32
    )
    total_rows = partial_logits.shape[0]
    seq_len = total_rows // NSEQ
    logits = lax.psum_scatter(partial_logits, "x", scatter_dimension=1, tiled=True)
    logits = lax.psum_scatter(logits, "yh", scatter_dimension=1, tiled=True)
    columns = logits.shape[1]
    soft = jax.nn.softplus(logits)
    act = jnp.log1p(soft)
    positions = jnp.arange(seq_len, dtype=jnp.int32)
    live = (positions[None, :] < lengths[:, None]).astype(jnp.float32)
    expo = jnp.exp(act / pool_temp).reshape(NSEQ, seq_len, columns) * live[:, :, None]
    totals = jnp.sum(expo, axis=1)
    pooled = pool_temp * jnp.log(totals)
    queries = pooled[:half]
    documents = pooled[half:]
    dots_part = lax.dot_general(
        queries, documents, (((1,), (1,)), ((), ())), precision=lax.Precision.HIGHEST
    )
    norms_part = jnp.sum(pooled * pooled, axis=1)
    stats = (dots_part, norms_part)
    for axis in ("c", "yl", "yh", "x", "z"):
        stats = lax.psum(stats, axis)
    dots, norms = stats
    inv = lax.rsqrt(norms + eps_norm)
    inv_q = inv[:half]
    inv_d = inv[half:]
    scores = dots * inv_q[:, None] * inv_d[None, :] / score_temp
    weights = jnp.exp(scores)
    row_sum = jnp.sum(weights, axis=1)
    probs = weights / row_sum[:, None]
    target = (jnp.arange(half, dtype=jnp.int32)[None, :] == pairing[:, None]).astype(jnp.float32)
    loss = jnp.sum(jnp.log(row_sum) - jnp.sum(scores * target, axis=1))
    dscore = grad_scale * (probs - target)
    gdots = dscore * inv_q[:, None] * inv_d[None, :] / score_temp
    dinv_q = jnp.sum(dscore * dots * inv_d[None, :], axis=1) / score_temp
    dinv_d = jnp.sum(dscore * dots * inv_q[:, None], axis=0) / score_temp
    dinv = jnp.concatenate([dinv_q, dinv_d])
    dnorm = -0.5 * dinv * inv * inv * inv
    dpool_q = (
        jnp.dot(gdots, documents, precision=lax.Precision.HIGHEST)
        + 2.0 * dnorm[:half, None] * queries
    )
    dpool_d = (
        jnp.dot(gdots.T, queries, precision=lax.Precision.HIGHEST)
        + 2.0 * dnorm[half:, None] * documents
    )
    dpooled = jnp.concatenate([dpool_q, dpool_d], axis=0)
    dact = (dpooled[:, None, :] * expo / totals[:, None, :]).reshape(total_rows, columns)
    dlogit = (dact * jax.nn.sigmoid(logits) / (1.0 + soft)).astype(jnp.bfloat16)
    dlogit = lax.all_gather(dlogit, SEC, axis=1, tiled=True)
    partial_grad = jnp.dot(dlogit, head_weight, preferred_element_type=jnp.float32)
    hidden_grad = lax.psum_scatter(partial_grad, "z", scatter_dimension=0, tiled=True)
    hidden_grad = lax.psum_scatter(hidden_grad, ("yl", "c"), scatter_dimension=0, tiled=True)
    return (hidden_grad, loss)


def solution(mesh):
    n_sec, n_voc = mesh.devices.shape
    fine = Mesh(mesh.devices.reshape(n_sec // 2, 2, n_voc // 4, 2, 2), SEC + VOC)
    in_specs = (P(VOC, SEC), P(VOC, SEC), P(), P())
    out_specs = (P(VOC, SEC), P())
    return jax.shard_map(local, mesh=fine, in_specs=in_specs, out_specs=out_specs, check_vma=False)
```

profile of v0, /device:TPU:1, one launch (start us, length us, event | category | flops | bytes accessed | tf_op | source)
XLA Modules:
  0.0 403.5 jit_solution(7920873863289771938)
XLA Ops:
  7.2 12.7 %all_gather.9 = bf16[32,1024]{1,0:T(8,128)(2,1)} all-gather(bf16[8,1024]{1,0:T(8,128)(2,1)} %param.4), channel_id=1, replica_groups=mesh['x'=4,'yh'=2,'z'=16,'yl'=2,'c'=2] {'yl','c'}, dimensions={0}, use_global_device_ids=true | all-gather | bytes 81920 | tf_op jit(solution)/shard_map/all_gather | solution.py:18
  20.0 60.9 %all-gather.3.cloned.1.call-done = bf16[512,1024]{1,0:T(8,128)(2,1)} async-done(((bf16[32,1024]{1,0:T(8,128)(2,1)}), bf16[512,1024]{1,0:T(8,128)(2,1)}) %all-gather.3.cloned.1.call-update) | async-done | bytes 1048592 | tf_op jit(solution)/shard_map/all_gather | solution.py:19
  81.0 4.7 %fusion.17 = f32[512,1536]{1,0:T(8,128)} fusion(bf16[512,1024]{1,0:T(8,128)(2,1)} %all-gather.3.cloned.1.call-done, bf16[1536,1024]{1,0:T(8,128)(2,1)S(1)} %copy-done), kind=kOutput, calls=%fused_computation.46 | convolution fusion | flops 1610612736 | bytes 7340032 | tf_op jit(solution)/shard_map/dot_general | solution.py:20
  85.8 52.5 %reduce-scatter.7.cloned.1.call-done = f32[512,384]{1,0:T(8,128)} async-done(((f32[512,1536]{1,0:T(8,128)}), f32[512,384]{1,0:T(8,128)}) %reduce-scatter.7.cloned.1.call-update) | async-done | bytes 786448 | tf_op jit(solution)/shard_map/reduce_scatter | solution.py:25
  138.3 2.3 copy.7
  140.6 0.0 all-gather.5.cloned.1.call-start
  140.6 0.1 fusion.3
  140.7 0.1 reshape.50
  140.8 29.2 %reduce-scatter.13.cloned.1.call-done = f32[192,512]{1,0:T(8,128)} async-done(((f32[384,512]{1,0:T(8,128)}), f32[192,512]{1,0:T(8,128)}) %reduce-scatter.13.cloned.1.call-update) | async-done | bytes 393232
  170.0 2.0 copy.8
  172.0 1.6 multiply_reduce_fusion
  173.6 0.1 multiply_reduce_fusion.1
  173.7 0.1 fusion.5
  173.9 2.8 all-reduce.2
  176.6 3.8 all-reduce.3
  180.4 5.3 %all-reduce.4 = (f32[8]{0:T(128)S(1)}, f32[4,4]{1,0:T(4,128)S(1)}) all-reduce(f32[8]{0:T(128)S(1)} %get-tuple-element.11, f32[4,4]{1,0:T(4,128)S(1)} %get-tuple-element.12), channel_id=1, replica_groups=mesh['x'=4,'yh'=2,'z'=16,'yl'=2,'c'=2] {'yh'}, use_global_device_ids=true, to_apply=%region_11.12 | all-reduce | flops 24 | bytes 192 | tf_op jit(solution)/shard_map/psum | solution.py:43
  185.7 8.7 %all-reduce.1 = (f32[8]{0:T(128)S(1)}, f32[4,4]{1,0:T(4,128)S(1)}) all-reduce(f32[8]{0:T(128)S(1)} %get-tuple-element.13, f32[4,4]{1,0:T(4,128)S(1)} %get-tuple-element.14), channel_id=1, replica_groups=mesh['x'=4,'yh'=2,'z'=16,'yl'=2,'c'=2] {'x'}, use_global_device_ids=true, to_apply=%region_12.13 | all-reduce | flops 24 | bytes 192 | tf_op jit(solution)/shard_map/psum | solution.py:43
  194.4 24.3 %all-reduce = (f32[8]{0:T(128)S(1)}, f32[4,4]{1,0:T(4,128)S(1)}) all-reduce(f32[8]{0:T(128)S(1)} %get-tuple-element.7, f32[4,4]{1,0:T(4,128)S(1)} %get-tuple-element.8), channel_id=1, replica_groups=mesh['x'=4,'yh'=2,'z'=16,'yl'=2,'c'=2] {'z'}, use_global_device_ids=true, to_apply=%region_13.14 | all-reduce | flops 24 | bytes 192 | tf_op jit(solution)/shard_map/psum | solution.py:43
  218.7 0.1 broadcast_multiply_fusion.2
  218.7 0.2 exponential_reduce_fusion
  218.9 0.2 multiply_reduce_fusion.3
  219.2 0.1 multiply_multiply_fusion.5
  219.2 0.1 slice_multiply_fusion.1
  219.3 0.2 convolution_add_fusion.1
  219.5 0.3 convolution_add_fusion
  219.8 1.7 fusion.2
  221.5 0.8 copy.6
  222.4 69.6 %all-gather.5.cloned.1.call-done = bf16[512,1536]{0,1:T(8,128)(2,1)} async-done(((bf16[512,192]{0,1:T(8,128)(2,1)}), bf16[512,1536]{0,1:T(8,128)(2,1)}) %all-gather.5.cloned.1.call-update) | async-done | bytes 1572880 | tf_op jit(solution)/shard_map/all_gather | solution.py:71
  292.0 4.6 %fusion.18 = f32[512,1024]{1,0:T(8,128)} fusion(bf16[512,1536]{0,1:T(8,128)(2,1)} %all-gather.5.cloned.1.call-done, bf16[1536,1024]{1,0:T(8,128)(2,1)S(1)} %copy-done), kind=kOutput, calls=%fused_computation.47 | convolution fusion | flops 1610612736 | bytes 6815744 | tf_op jit(solution)/shard_map/dot_general | solution.py:72
  296.6 63.7 %reduce-scatter.9.cloned.1.call-done = f32[32,1024]{1,0:T(8,128)} async-done(((f32[512,1024]{1,0:T(8,128)}), f32[32,1024]{1,0:T(8,128)}) %reduce-scatter.9.cloned.1.call-update) | async-done | bytes 131088 | tf_op jit(solution)/shard_map/reduce_scatter | solution.py:73
  360.3 0.6 subtract_reduce_fusion
  360.9 35.8 %reduce-scatter.11.cloned.1.call-done = f32[8,1024]{1,0:T(8,128)} async-done(((f32[32,1024]{1,0:T(8,128)}), f32[8,1024]{1,0:T(8,128)}) %reduce-scatter.11.cloned.1.call-update) | async-done | bytes 32784 | tf_op jit(solution)/shard_map/reduce_scatter | solution.py:74
  (20 shorter events, 0.4 us)
Async XLA Ops:
  7.2 73.8 %copy-start = (bf16[1536,1024]{1,0:T(8,128)(2,1)S(1)}, bf16[1536,1024]{1,0:T(8,128)(2,1)}, u32[]{:S(2)}) copy-start(bf16[1536,1024]{1,0:T(8,128)(2,1)} %param.5) | copy-start | bytes 9437188
  7.2 73.8 %all-gather.3.cloned.1.call-start = ((), (), s32[]{:S(2)}) async-start(), calls=%async_computation.4 | async-start | bytes 1114112 | tf_op jit(solution)/shard_map/all_gather | solution.py:19
  20.0 118.3 %reduce-scatter.7.cloned.1.call-start = ((), (), s32[]{:S(2)}) async-start(), calls=%async_computation.5 | async-start | bytes 3932160 | tf_op jit(solution)/shard_map/reduce_scatter | solution.py:25
  85.7 54.9 %copy-start.1 = (s32[8]{0:T(128)S(1)}, s32[8]{0:T(128)}, u32[]{:S(2)}) copy-start(s32[8]{0:T(128)} %param.6) | copy-start | bytes 100
  85.7 133.2 %copy-start.2 = (s32[4]{0:T(128)S(1)}, s32[4]{0:T(128)}, u32[]{:S(2)}) copy-start(s32[4]{0:T(128)} %param.7) | copy-start | bytes 52
  85.7 84.3 %reduce-scatter.13.cloned.1.call-start = ((), (), s32[]{:S(2)}) async-start(), calls=%async_computation.9 | async-start | bytes 1179648
  140.6 151.4 %all-gather.5.cloned.1.call-start = ((), (), s32[]{:S(2)}) async-start(), calls=%async_computation.6 | async-start | bytes 1769472 | tf_op jit(solution)/shard_map/all_gather | solution.py:71
  222.3 137.9 %reduce-scatter.9.cloned.1.call-start = ((), (), s32[]{:S(2)}) async-start(), calls=%async_computation.7 | async-start | bytes 2228224 | tf_op jit(solution)/shard_map/reduce_scatter | solution.py:73
  296.6 100.1 %reduce-scatter.11.cloned.1.call-start = ((), (), s32[]{:S(2)}) async-start(), calls=%async_computation.8 | async-start | bytes 163840 | tf_op jit(solution)/shard_map/reduce_scatter | solution.py:74
Sparse Core Ops, SparseCore 0:
  20.1 60.8 all-gather.2
  85.9 52.3 reduce-scatter.6
  141.1 28.9 reduce-scatter.12
  222.5 69.4 all-gather.4
  296.7 63.5 reduce-scatter.8
  363.7 32.9 reduce-scatter.10
where the time goes:
time: 404 us
  waiting for transfers between devices  312 us (77%)
  blocking collectives  57.5 us (14%)
  between operations  14.2 us (4%)
  matrix products  9.88 us (2%)
  local copies, waits for them, and re-layouts  5.15 us (1%)
  other arithmetic  4.75 us (1%)
    all_gather x1, waiting for transfers between devices, local(): dlogit = lax.all_gather(dlogit, SEC, axis=1, tiled=True)  69.6 us
    reduce_scatter x1, waiting for transfers between devices, local(): lax.psum_scatter(partial_grad, 'z', scatter_dimension=0, tiled=True)  63.7 us
    all_gather x1, waiting for transfers between devices, local(): gathered = lax.all_gather(gathered, 'z', axis=0, tiled=True)  60.9 us
    reduce_scatter x1, waiting for transfers between devices, local(): lax.psum_scatter(partial_logits, 'x', scatter_dimension=1, tiled=True)  52.5 us
    psum x5, blocking collectives, local(): stats = lax.psum(stats, axis)  44.8 us
    reduce_scatter x1, waiting for transfers between devices, local(): lax.psum_scatter(hidden_grad, ('yl', 'c'), scatter_dimension=0, tiled=True)  35.8 us
    unnamed x7, waiting for transfers between devices  29.3 us
    all_gather x1, blocking collectives, local(): gathered = lax.all_gather(hidden, ('yl', 'c'), axis=0, tiled=True)  12.7 us
  transfers between devices with their start and end apart: 6, of which 6 were waited for; matrix products, arithmetic and copies ran while one was open for 0% of the time, Pallas kernels for 0%

commit v1 on v0

--- a/solution.py
+++ b/solution.py
@@ -11,6 +11,13 @@
 eps_norm = 1e-06
 SEC = ("x", "yh")
 VOC = ("z", "yl", "c")
+
+
+def point_yards(state):
+    u1 = lax.all_to_all(
+        jnp.stack([state] * lax.axis_size(SEC), axis=0), axis_name=SEC, split_axis=0, concat_axis=0
+    )
+    return jnp.concatenate(u1, 1)
 
 
 def local(hidden, head_weight, lengths, pairing):
@@ -68,7 +75,7 @@
     dpooled = jnp.concatenate([dpool_q, dpool_d], axis=0)
     dact = (dpooled[:, None, :] * expo / totals[:, None, :]).reshape(total_rows, columns)
     dlogit = (dact * jax.nn.sigmoid(logits) / (1.0 + soft)).astype(jnp.bfloat16)
-    dlogit = lax.all_gather(dlogit, SEC, axis=1, tiled=True)
+    dlogit = point_yards(dlogit)
     partial_grad = jnp.dot(dlogit, head_weight, preferred_element_type=jnp.float32)
     hidden_grad = lax.psum_scatter(partial_grad, "z", scatter_dimension=0, tiled=True)
     hidden_grad = lax.psum_scatter(hidden_grad, ("yl", "c"), scatter_dimension=0, tiled=True)

time: 404 us -> 356 us (0.88)
  waiting for transfers between devices: 312 us -> 248 us
  blocking collectives: 57.5 us -> 74.3 us
    all_gather x1 -> x0, waiting for transfers between devices: 69.6 us -> none  [local(): dlogit = lax.all_gather(dlogit, SEC, axis=1, tiled=True)]
    all_to_all x0 -> x1, blocking collectives: none -> 16.7 us  [point_yards(): lax.all_to_all(jnp.stack([state] * lax.axis_size(SEC), axis=0), axis_name...]
    reduce_scatter x1, waiting for transfers between devices: 63.7 us -> 69 us  [local(): lax.psum_scatter(partial_grad, 'z', scatter_dimension=0, tiled=True)]
    unnamed x7 -> x6, waiting for transfers between devices: 29.3 us -> 29.3 us
  transfers between devices with their start and end apart: 6 -> 5, of which waited for: 6 -> 5; matrix products, arithmetic and copies ran while one was open for 0% -> 0% of each run, Pallas kernels for 0% -> 0%
where the time goes in v1:
time: 356 us; the launch traced here: 355 us
  waiting for transfers between devices  248 us (70%)
  blocking collectives  74.3 us (21%)
  between operations  13.8 us (4%)
  matrix products  8.51 us (2%)
  local copies, waits for them, and re-layouts  5.56 us (2%)
  other arithmetic  5.45 us (2%)
    reduce_scatter x1, waiting for transfers between devices, local(): lax.psum_scatter(partial_grad, 'z', scatter_dimension=0, tiled=True)  69 us
    all_gather x1, waiting for transfers between devices, local(): gathered = lax.all_gather(gathered, 'z', axis=0, tiled=True)  60.9 us
    reduce_scatter x1, waiting for transfers between devices, local(): lax.psum_scatter(partial_logits, 'x', scatter_dimension=1, tiled=True)  52.5 us
    psum x5, blocking collectives, local(): stats = lax.psum(stats, axis)  44.8 us
    reduce_scatter x1, waiting for transfers between devices, local(): lax.psum_scatter(hidden_grad, ('yl', 'c'), scatter_dimension=0, tiled=True)  35.8 us
    unnamed x6, waiting for transfers between devices  29.3 us
    all_to_all x1, blocking collectives, point_yards(): lax.all_to_all(jnp.stack([state] * lax.axis_size(SEC), axis=0), axis_name...  16.7 us
    all_gather x1, blocking collectives, local(): gathered = lax.all_gather(hidden, ('yl', 'c'), axis=0, tiled=True)  12.7 us
  transfers between devices with their start and end apart: 5, of which 5 were waited for; matrix products, arithmetic and copies ran while one was open for 0% of the time, Pallas kernels for 0%

profile of v1, /device:TPU:1, one launch (start us, length us, event | category | flops | bytes accessed | tf_op | source)
XLA Modules:
  0.0 355.4 jit_solution(3072520995899389020)
XLA Ops:
  7.2 12.7 %all_gather.6 = bf16[32,1024]{1,0:T(8,128)(2,1)} all-gather(bf16[8,1024]{1,0:T(8,128)(2,1)} %param.4), channel_id=1, replica_groups=mesh['x'=4,'yh'=2,'z'=16,'yl'=2,'c'=2] {'yl','c'}, dimensions={0}, use_global_device_ids=true | all-gather | bytes 81920 | tf_op jit(solution)/shard_map/all_gather | solution.py:25
  20.0 60.9 %all-gather.2.cloned.1.call-done = bf16[512,1024]{1,0:T(8,128)(2,1)} async-done(((bf16[32,1024]{1,0:T(8,128)(2,1)}), bf16[512,1024]{1,0:T(8,128)(2,1)}) %all-gather.2.cloned.1.call-update) | async-done | bytes 1048592 | tf_op jit(solution)/shard_map/all_gather | solution.py:26
  81.0 4.7 %fusion.17 = f32[512,1536]{1,0:T(8,128)} fusion(bf16[512,1024]{1,0:T(8,128)(2,1)} %all-gather.2.cloned.1.call-done, bf16[1536,1024]{1,0:T(8,128)(2,1)S(1)} %copy-done), kind=kOutput, calls=%fused_computation.46 | convolution fusion | flops 1610612736 | bytes 7340032 | tf_op jit(solution)/shard_map/dot_general | solution.py:27
  85.8 52.5 %reduce-scatter.7.cloned.1.call-done = f32[512,384]{1,0:T(8,128)} async-done(((f32[512,1536]{1,0:T(8,128)}), f32[512,384]{1,0:T(8,128)}) %reduce-scatter.7.cloned.1.call-update) | async-done | bytes 786448 | tf_op jit(solution)/shard_map/reduce_scatter | solution.py:32
  138.3 2.3 copy.8
  140.6 0.1 fusion.3
  140.7 0.1 reshape.60
  140.8 29.2 %reduce-scatter.13.cloned.1.call-done = f32[192,512]{1,0:T(8,128)} async-done(((f32[384,512]{1,0:T(8,128)}), f32[192,512]{1,0:T(8,128)}) %reduce-scatter.13.cloned.1.call-update) | async-done | bytes 393232
  170.0 2.0 copy.9
  172.0 1.6 multiply_reduce_fusion
  173.6 0.1 multiply_reduce_fusion.1
  173.7 0.1 fusion.5
  173.9 2.8 all-reduce.2
  176.6 3.8 %all-reduce.3 = (f32[8]{0:T(128)S(1)}, f32[4,4]{1,0:T(4,128)S(1)}) all-reduce(f32[8]{0:T(128)S(1)} %get-tuple-element.9, f32[4,4]{1,0:T(4,128)S(1)} %get-tuple-element.10), channel_id=1, replica_groups=mesh['x'=4,'yh'=2,'z'=16,'yl'=2,'c'=2] {'yl'}, use_global_device_ids=true, to_apply=%region_10.11 | all-reduce | flops 24 | bytes 192 | tf_op jit(solution)/shard_map/psum | solution.py:50
  180.4 5.3 %all-reduce.4 = (f32[8]{0:T(128)S(1)}, f32[4,4]{1,0:T(4,128)S(1)}) all-reduce(f32[8]{0:T(128)S(1)} %get-tuple-element.11, f32[4,4]{1,0:T(4,128)S(1)} %get-tuple-element.12), channel_id=1, replica_groups=mesh['x'=4,'yh'=2,'z'=16,'yl'=2,'c'=2] {'yh'}, use_global_device_ids=true, to_apply=%region_11.12 | all-reduce | flops 24 | bytes 192 | tf_op jit(solution)/shard_map/psum | solution.py:50
  185.7 8.7 %all-reduce.1 = (f32[8]{0:T(128)S(1)}, f32[4,4]{1,0:T(4,128)S(1)}) all-reduce(f32[8]{0:T(128)S(1)} %get-tuple-element.13, f32[4,4]{1,0:T(4,128)S(1)} %get-tuple-element.14), channel_id=1, replica_groups=mesh['x'=4,'yh'=2,'z'=16,'yl'=2,'c'=2] {'x'}, use_global_device_ids=true, to_apply=%region_12.13 | all-reduce | flops 24 | bytes 192 | tf_op jit(solution)/shard_map/psum | solution.py:50
  194.4 24.3 %all-reduce = (f32[8]{0:T(128)S(1)}, f32[4,4]{1,0:T(4,128)S(1)}) all-reduce(f32[8]{0:T(128)S(1)} %get-tuple-element.7, f32[4,4]{1,0:T(4,128)S(1)} %get-tuple-element.8), channel_id=1, replica_groups=mesh['x'=4,'yh'=2,'z'=16,'yl'=2,'c'=2] {'z'}, use_global_device_ids=true, to_apply=%region_13.14 | all-reduce | flops 24 | bytes 192 | tf_op jit(solution)/shard_map/psum | solution.py:50
  218.7 0.1 broadcast_multiply_fusion.2
  218.7 0.2 exponential_reduce_fusion
  218.9 0.2 multiply_reduce_fusion.3
  219.2 0.1 multiply_multiply_fusion.5
  219.2 0.1 slice_multiply_fusion.1
  219.3 0.2 convolution_add_fusion.1
  219.5 0.3 convolution_add_fusion
  219.8 2.4 fusion.2
  222.2 1.1 copy.7
  223.3 0.1 stack.2
  223.4 16.7 %all_to_all.5 = bf16[8,512,192]{1,2,0:T(8,128)(2,1)S(1)} all-to-all(bf16[8,512,192]{1,2,0:T(8,128)(2,1)S(1)} %stack.2), channel_id=1, replica_groups=mesh['x'=4,'yh'=2,'z'=16,'yl'=2,'c'=2] {'x','yh'}, dimensions={0} | all-to-all | bytes 3145728 | tf_op jit(solution)/shard_map/all_to_all | solution.py:17
  240.2 3.2 fusion.18
  243.5 69.0 %reduce-scatter.9.cloned.1.call-done = f32[32,1024]{1,0:T(8,128)} async-done(((f32[512,1024]{1,0:T(8,128)}), f32[32,1024]{1,0:T(8,128)}) %reduce-scatter.9.cloned.1.call-update) | async-done | bytes 131088 | tf_op jit(solution)/shard_map/reduce_scatter | solution.py:80
  312.4 0.6 subtract_reduce_fusion
  313.1 35.8 %reduce-scatter.11.cloned.1.call-done = f32[8,1024]{1,0:T(8,128)} async-done(((f32[32,1024]{1,0:T(8,128)}), f32[8,1024]{1,0:T(8,128)}) %reduce-scatter.11.cloned.1.call-update) | async-done | bytes 32784 | tf_op jit(solution)/shard_map/reduce_scatter | solution.py:81
  (19 shorter events, 0.3 us)
Async XLA Ops:
  7.2 73.8 %copy-start = (bf16[1536,1024]{1,0:T(8,128)(2,1)S(1)}, bf16[1536,1024]{1,0:T(8,128)(2,1)}, u32[]{:S(2)}) copy-start(bf16[1536,1024]{1,0:T(8,128)(2,1)} %param.5) | copy-start | bytes 9437188
  7.2 73.8 %all-gather.2.cloned.1.call-start = ((), (), s32[]{:S(2)}) async-start(), calls=%async_computation.5 | async-start | bytes 1114112 | tf_op jit(solution)/shard_map/all_gather | solution.py:26
  20.0 118.3 %reduce-scatter.7.cloned.1.call-start = ((), (), s32[]{:S(2)}) async-start(), calls=%async_computation.6 | async-start | bytes 3932160 | tf_op jit(solution)/shard_map/reduce_scatter | solution.py:32
  85.7 54.9 %copy-start.1 = (s32[8]{0:T(128)S(1)}, s32[8]{0:T(128)}, u32[]{:S(2)}) copy-start(s32[8]{0:T(128)} %param.6) | copy-start | bytes 100
  85.7 133.2 %copy-start.2 = (s32[4]{0:T(128)S(1)}, s32[4]{0:T(128)}, u32[]{:S(2)}) copy-start(s32[4]{0:T(128)} %param.7) | copy-start | bytes 52
  85.7 84.3 %reduce-scatter.13.cloned.1.call-start = ((), (), s32[]{:S(2)}) async-start(), calls=%async_computation.9 | async-start | bytes 1179648
  140.6 171.8 %reduce-scatter.9.cloned.1.call-start = ((), (), s32[]{:S(2)}) async-start(), calls=%async_computation.7 | async-start | bytes 2228224 | tf_op jit(solution)/shard_map/reduce_scatter | solution.py:80
  243.4 105.5 %reduce-scatter.11.cloned.1.call-start = ((), (), s32[]{:S(2)}) async-start(), calls=%async_computation.8 | async-start | bytes 163840 | tf_op jit(solution)/shard_map/reduce_scatter | solution.py:81
Sparse Core Ops, SparseCore 0:
  20.1 60.8 all-gather.1
  85.9 52.3 reduce-scatter.6
  141.1 28.9 reduce-scatter.12
  243.5 68.8 reduce-scatter.8
  315.9 32.9 reduce-scatter.10
